TPU v7x, 512 devices: a whole 4x4x16 slice. The times are simulated.
512 devices in a mesh: dp: 4 (over x), ctx: 16 (over z), mp: 8 (over y, core).
Axes of the slice: x: 4, y: 4, z: 16, core: 2. Of those that a mesh axis runs over, the one named last changes fastest.
Arguments:
- tokens: bfloat16 [4, 2048, 4096], P('dp', 'ctx'), may hold values from -52 to 52
- x_weight: bfloat16 [4096, 8192], P(('dp', 'ctx'), 'mp'), may hold values from -0.09375 to 0.09375
- bc_weight: bfloat16 [4096, 1024], P(('dp', 'ctx'), 'mp'), may hold values from -0.09375 to 0.09375
- dt_weight: bfloat16 [4096, 128], P(('dp', 'ctx'), 'mp'), may hold values from -0.0234375 to 0.0234375
- conv_x: float32 [5, 8192], P(None, 'mp'), may hold values from -0.5 to 0.5
- conv_bc: float32 [5, 1024], P(None, 'mp'), may hold values from -0.5 to 0.5
- dt_bias: float32 [128], P('mp'), may hold values from -4.5 to -2.5
- a_log: float32 [128], P('mp')
- d_skip: float32 [128], P('mp'), may hold values from 0.5 to 1.5
- norm_gain: float32 [8192], P('mp'), may hold values from 0.5 to 1.5
Outputs:
- mixer_out: bfloat16 [4, 2048, 8192], P('dp', 'ctx', 'mp')
- kurtosis: float32 [4096], P('mp')
All inputs are finite; a program needn't handle non-finite values.
Results may differ from a plain program's by a relative error of at most 0.015.
Values may be sent and summed in bfloat16 or wider, within the bound.
No kernel may reach another device: no remote copies, remote signals or barrier semaphores. Data moves between devices by JAX's collectives and lax.ppermute only.
A program may use at most 64 MiB of HBM per device.

v0:
```python
import jax
import jax.numpy as jnp
from jax import lax
from jax.sharding import PartitionSpec as P

ROOT = 64
HEADS = 128
G = 4
NS = 128
HIGH = lax.Precision.HIGHEST
CTX = ("ch", "cl")


def passed_along(value, axis, steps, count):
    first, last = (max(0, -steps), min(count, count - steps))
    return lax.ppermute(value, axis, [(source, source + steps) for source in range(first, last)])


def decay_products(row_decay, targets):
    count = row_decay.shape[0]
    target = lax.broadcasted_iota(jnp.int32, (targets, count, count), 0)
    source = lax.broadcasted_iota(jnp.int32, (targets, count, count), 1)
    between = lax.broadcasted_iota(jnp.int32, (targets, count, count), 2)
    inside = jnp.logical_and(between > source, between < target)
    factors = jnp.where(inside[..., None], row_decay[None, None], 1.0)
    products = jnp.prod(factors, 2)
    return jnp.where((source[:, :, 0] < target[:, :, 0])[..., None], products, 0.0)


def entering(decay, contrib):
    quads, quad = (lax.axis_index("ch"), lax.axis_size("cl"))
    place = lax.axis_index("cl")
    lanes = contrib.shape[-1]
    head_rows = contrib.shape[-2]
    heads = decay.size
    chunk = contrib.size // lanes // quad
    pieces = contrib.reshape(quad, chunk, lanes)
    tail = jnp.zeros((quad, 8, lanes), jnp.float32)
    tail = tail.at[:, 0, :heads].set(jnp.broadcast_to(decay.reshape(1, heads), (quad, heads)))
    outgoing = jnp.concatenate([pieces, tail], 1).astype(jnp.bfloat16)
    incoming = lax.all_to_all(outgoing, "cl", 0, 0).astype(jnp.float32)
    states = incoming[:, :chunk]
    decays = incoming[:, chunk, :heads]
    row_head = (place * chunk + lax.broadcasted_iota(jnp.int32, (chunk, heads), 0)) // head_rows
    pick = row_head == lax.broadcasted_iota(jnp.int32, (chunk, heads), 1)
    row_decay = jnp.sum(jnp.where(pick[None], decays[:, None, :], 0.0), -1)
    local = jnp.einsum("kjr,jrl->krl", decay_products(row_decay, quad + 1), states, precision=HIGH)
    step = lax.broadcasted_iota(jnp.int32, (quad + 1, quad, chunk), 0)
    index = lax.broadcasted_iota(jnp.int32, (quad + 1, quad, chunk), 1)
    entry = jnp.prod(jnp.where(index < step, row_decay[None], 1.0), 1)
    pad_rows = 8 - chunk // lanes % 8
    summary = jnp.concatenate(
        [local[quad], entry[quad].reshape(chunk // lanes, lanes), jnp.zeros((pad_rows, lanes))]
    )
    count_hi = lax.axis_size("ch")
    shared = lax.all_gather(summary.astype(jnp.bfloat16), "ch").astype(jnp.float32)
    totals = shared[:, :chunk]
    quad_decay = shared[:, chunk : chunk + chunk // lanes].reshape(count_hi, chunk)
    earlier = lax.broadcasted_iota(jnp.int32, (count_hi, count_hi, chunk), 0)
    middle = lax.broadcasted_iota(jnp.int32, (count_hi, count_hi, chunk), 1)
    spans = jnp.logical_and(middle > earlier, middle < quads)
    across = jnp.prod(jnp.where(spans, quad_decay[None], 1.0), 1)
    across = jnp.where(earlier[:, 0] < quads, across, 0.0)
    entering_state = jnp.einsum("qr,qrl->rl", across, totals, precision=HIGH)
    carried = local[:quad] + entry[:quad, :, None] * entering_state[None]
    returned = lax.all_to_all(carried.astype(jnp.bfloat16), "cl", 0, 0)
    return returned.astype(jnp.float32).reshape(contrib.shape)


def hadamard_signs(sign_order):
    row_index = lax.broadcasted_iota(jnp.int32, (sign_order, sign_order), 0)
    col_index = lax.broadcasted_iota(jnp.int32, (sign_order, sign_order), 1)
    common = jnp.bitwise_and(row_index, col_index)
    parity = jnp.zeros((sign_order, sign_order), jnp.int32)
    for bit_index in range(sign_order.bit_length() - 1):
        parity = parity + jnp.bitwise_and(jnp.right_shift(common, bit_index), 1)
    return 1.0 - 2.0 * jnp.bitwise_and(parity, 1).astype(jnp.float32)


def kurtosis_from(powers, row_count):
    average = powers[0] / row_count
    second = powers[1] / row_count - average * average
    fourth = (
        powers[3] / row_count
        - 4.0 * average * powers[2] / row_count
        + 6.0 * average * average * powers[1] / row_count
        - 3.0 * average * average * average * average
    )
    return fourth / (second * second + 1e-06)


def shards(
    tokens, x_weight, bc_weight, dt_weight, conv_x, conv_bc, dt_bias, a_log, d_skip, norm_gain
):
    tok_rows = tokens.shape[1]
    model_width = tokens.shape[2]
    signs = hadamard_signs(ROOT)
    blocks = tokens.reshape(tok_rows, ROOT, ROOT)
    first_pass = jnp.einsum(
        "tab,ac->tcb", blocks, signs.astype(jnp.bfloat16), preferred_element_type=jnp.float32
    )
    second = jnp.einsum("tcb,bd->tcd", first_pass, signs, precision=HIGH)
    rotated = (second.reshape(tok_rows, model_width) / ROOT).astype(jnp.bfloat16)
    channel_share = model_width // lax.axis_size("mp")
    own_cols = lax.dynamic_slice_in_dim(
        rotated, lax.axis_index("mp") * channel_share, channel_share, 1
    ).astype(jnp.float32)
    square = own_cols * own_cols
    powers = jnp.stack(
        [
            jnp.sum(own_cols, 0),
            jnp.sum(square, 0),
            jnp.sum(square * own_cols, 0),
            jnp.sum(square * square, 0),
        ]
    )
    ctx_count = lax.axis_size("ch") * lax.axis_size("cl")
    row_count = float(tok_rows * lax.axis_size("dp") * ctx_count)
    totals = lax.psum(lax.psum(powers, CTX), "dp")
    totals, rotated = lax.optimization_barrier((totals, rotated))
    kurtosis = kurtosis_from(totals, row_count)
    local_panel = jnp.concatenate([x_weight, bc_weight, dt_weight], 1)
    panel = lax.all_gather(local_panel, CTX, axis=0, tiled=True)
    seqs = lax.axis_size("dp")
    share = model_width // seqs
    rim = 8
    earlier = passed_along(rotated[tok_rows - rim :], CTX, 1, ctx_count)
    extended = jnp.concatenate([earlier, rotated], 0)
    outgoing = extended.reshape(tok_rows + rim, seqs, share).transpose(1, 0, 2)
    incoming = lax.all_to_all(outgoing, "dp", 0, 0)
    x_end = x_weight.shape[1]
    bc_end = x_end + bc_weight.shape[1]
    side_partials = jnp.einsum(
        "kti,io->kto", incoming, panel[:, x_end:], preferred_element_type=jnp.float32
    )
    side_back = lax.all_to_all(side_partials.astype(jnp.bfloat16), "dp", 0, 0)
    x_partials = jnp.einsum(
        "kti,io->kto", incoming, panel[:, :x_end], preferred_element_type=jnp.float32
    )
    x_back = lax.all_to_all(x_partials.astype(jnp.bfloat16), "dp", 0, 0)
    side_ext = jnp.sum(side_back.astype(jnp.float32), 0)
    x_ext = jnp.sum(x_back.astype(jnp.float32), 0)
    x_cols = x_end
    bc_width = bc_end - x_end
    dt_proj = lax.optimization_barrier(side_ext[rim:, bc_width:].astype(jnp.bfloat16))
    kernel = conv_x.shape[0] - 1

    def causal_conv(rows, taps):
        padded = rows.astype(jnp.bfloat16)[rim - (kernel - 1) :]
        total = taps[kernel]
        for tap_index in range(kernel):
            total = total + taps[tap_index] * padded[tap_index : tap_index + tok_rows]
        return jax.nn.silu(total).astype(jnp.bfloat16)

    bc_own = causal_conv(side_ext[:, :bc_width], conv_bc)
    x_conv = causal_conv(x_ext, conv_x)
    heads_dev = dt_weight.shape[1]
    head_size = x_cols // heads_dev
    per_group = HEADS // G
    groups_here = max(1, heads_dev // per_group)
    heads_local = heads_dev // groups_here
    first_group = lax.axis_index("mp") * heads_dev // per_group
    mp_count = lax.axis_size("mp")
    if bc_own.shape[1] == NS and mp_count == 2 * G and (groups_here == 1):
        owner = [m * heads_dev // per_group for m in range(mp_count)]
        odd_first = [(owner[m] if m % 2 == 0 else G + owner[m], m) for m in range(mp_count)]
        even_first = [(G + owner[m] if m % 2 == 0 else owner[m], m) for m in range(mp_count)]
        got_a = lax.ppermute(bc_own, "mp", odd_first)
        got_b = lax.ppermute(bc_own, "mp", even_first)
        even = lax.axis_index("mp") % 2 == 0
        write_here = jnp.where(even, got_a, got_b).reshape(tok_rows, 1, NS)
        read_here = jnp.where(even, got_b, got_a).reshape(tok_rows, 1, NS)
    else:
        group_all = lax.all_gather(bc_own, "mp", axis=1, tiled=True)
        write_all = group_all[:, : G * NS].reshape(tok_rows, G, NS)
        read_all = group_all[:, G * NS :].reshape(tok_rows, G, NS)
        write_here = lax.dynamic_slice_in_dim(write_all, first_group, groups_here, 1)
        read_here = lax.dynamic_slice_in_dim(read_all, first_group, groups_here, 1)
    step_size = jax.nn.softplus(dt_proj.astype(jnp.float32) + dt_bias)
    decay_rate = step_size * jnp.exp(a_log)
    cumulative = jnp.cumsum(decay_rate, 0)
    block_end = cumulative[-1]
    causal = lax.broadcasted_iota(jnp.int32, (tok_rows, tok_rows), 0) >= lax.broadcasted_iota(
        jnp.int32, (tok_rows, tok_rows), 1
    )
    spread = cumulative.T[:, :, None] - cumulative.T[:, None, :]
    decay_mask = jnp.where(causal, jnp.exp(-jnp.where(causal, spread, 0.0)), 0.0)
    scores = jnp.einsum("tgn,sgn->gts", read_here, write_here, preferred_element_type=jnp.float32)
    weights = (
        scores[:, None]
        * decay_mask.reshape(groups_here, heads_local, tok_rows, tok_rows)
        * step_size.T.reshape(groups_here, heads_local, 1, tok_rows)
    ).astype(jnp.bfloat16)
    x_heads = x_conv.reshape(tok_rows, groups_here, heads_local, head_size)
    within_block = jnp.einsum(
        "ghts,sghp->tghp", weights, x_heads, preferred_element_type=jnp.float32
    )
    update = (
        (jnp.exp(-(block_end - cumulative)) * step_size).reshape(
            tok_rows, groups_here, heads_local
        )[..., None]
        * x_heads
    ).astype(jnp.bfloat16)
    contrib = jnp.einsum("sghp,sgn->ghpn", update, write_here, preferred_element_type=jnp.float32)
    carried = entering(jnp.exp(-block_end).reshape(groups_here, heads_local), contrib)
    from_before = jnp.exp(-cumulative).reshape(tok_rows, groups_here, heads_local)[
        ..., None
    ] * jnp.einsum("tgn,ghpn->tghp", read_here.astype(jnp.float32), carried, precision=HIGH)
    output_raw = (
        within_block
        + from_before
        + d_skip.reshape(groups_here, heads_local)[None, :, :, None] * x_heads.astype(jnp.float32)
    )
    mean_square = jnp.mean(output_raw * output_raw, -1, keepdims=True)
    normed = (
        output_raw
        * lax.rsqrt(mean_square + 1e-05)
        * norm_gain.reshape(groups_here, heads_local, head_size)
    )
    return (normed.reshape(1, tok_rows, x_cols).astype(jnp.bfloat16), kurtosis)


def solution(mesh):
    grid = mesh.devices
    quad = 4 if grid.shape[1] % 4 == 0 else 1
    split = jax.sharding.Mesh(
        grid.reshape(grid.shape[0], grid.shape[1] // quad, quad, grid.shape[2]),
        ("dp", "ch", "cl", "mp"),
    )
    return jax.shard_map(
        shards,
        mesh=split,
        in_specs=(
            P("dp", CTX, None),
            P(("dp",) + CTX, "mp"),
            P(("dp",) + CTX, "mp"),
            P(("dp",) + CTX, "mp"),
            P(None, "mp"),
            P(None, "mp"),
            P("mp"),
            P("mp"),
            P("mp"),
            P("mp"),
        ),
        out_specs=(P("dp", CTX, "mp"), P("mp")),
        check_vma=False,
    )
```

profile of v0, /device:TPU:12, one launch (start us, length us, event | category | flops | bytes accessed | tf_op | source)
XLA Modules:
  0.0 176.9 jit_solution(554264727969521265)
XLA Ops:
  8.0 1.6 pad_maximum_fusion.2
  9.6 1.6 copy.123
  12.1 3.3 %multiply_convert_fusion = bf16[128,64,64]{0,2,1:T(8,128)(2,1)S(1)} fusion(f32[128,64,64]{0,1,2:T(8,128)S(1)} %convolution_bitcast_fusion), kind=kOutput, calls=%fused_computation.4 | convolution fusion | flops 403791872 | bytes 3145728 | tf_op jit(solution)/shard_map/tcb,bd->tcd/dot_general | solution.py:102
  15.8 37.2 %psum.14 = f32[4,512]{1,0:T(4,128)S(1)} all-reduce(f32[4,512]{1,0:T(4,128)S(1)} %pad_maximum_fusion.3), channel_id=1, replica_groups=mesh['dp'=4,'ch'=4,'cl'=4,'mp'=8] {'ch','cl'}, use_global_device_ids=true, to_apply=%region_4.0 | all-reduce | flops 2048 | bytes 16384 | tf_op jit(solution)/shard_map/psum | solution.py:119
  53.1 8.5 %psum.15 = f32[4,512]{1,0:T(4,128)S(1)} all-reduce(f32[4,512]{1,0:T(4,128)S(1)} %psum.14), channel_id=1, replica_groups=mesh['dp'=4,'ch'=4,'cl'=4,'mp'=8] {'dp'}, use_global_device_ids=true, to_apply=%region_5.0 | all-reduce | flops 2048 | bytes 16384 | tf_op jit(solution)/shard_map/psum | solution.py:119
  62.1 1.7 collective-permute-start
  63.7 2.6 %collective-permute-done = bf16[8,4096]{1,0:T(8,128)(2,1)S(1)} collective-permute-done((bf16[8,4096]{1,0:T(8,128)(2,1)S(1)}, bf16[8,4096]{1,0:T(8,128)(2,1)S(1)}, u32[]{:S(2)}, u32[]{:S(2)}) %collective-permute-start) | collective-permute-done | bytes 65568 | tf_op jit(solution)/shard_map/ppermute | solution.py:16
  66.5 1.1 copy.166
  67.6 5.8 %all-to-all-start = ((bf16[4,136,1024]{2,1,0:T(8,128)(2,1)}), bf16[4,136,1024]{2,1,0:T(8,128)(2,1)S(1)}, u32[]{:S(2)}, u32[]{:S(2)}) async-start(bf16[4,136,1024]{2,1,0:T(8,128)(2,1)} %bitcast.108), calls=%async_computation | async-start | bytes 2228224 | tf_op jit(solution)/shard_map/all_to_all | solution.py:130
  73.5 8.2 %all-to-all-done = bf16[4,136,1024]{2,1,0:T(8,128)(2,1)S(1)} async-done(((bf16[4,136,1024]{2,1,0:T(8,128)(2,1)}), bf16[4,136,1024]{2,1,0:T(8,128)(2,1)S(1)}, u32[]{:S(2)}, u32[]{:S(2)}) %all-to-all-start) | async-done | bytes 1114144 | tf_op jit(solution)/shard_map/all_to_all | solution.py:130
  81.7 8.6 %all-gather.2.cloned.1.call-done = bf16[1024,1168]{1,0:T(8,128)(2,1)} async-done(((bf16[64,1168]{1,0:T(8,128)(2,1)}), bf16[1024,1168]{1,0:T(8,128)(2,1)}) %all-gather.2.cloned.1.call-update) | async-done | bytes 2392080 | tf_op jit(solution)/shard_map/all_gather | solution.py:123
  90.3 2.2 %convolution_convert_fusion = bf16[4,136,144]{2,1,0:T(8,128)(2,1)} fusion(bf16[4,136,1024]{2,1,0:T(8,128)(2,1)S(1)} %all-to-all-done, bf16[1024,1168]{1,0:T(8,128)(2,1)} %all-gather.2.cloned.1.call-done), kind=kOutput, calls=%fused_computation.13 | convolution fusion | flops 160510464 | bytes 1795072 | tf_op jit(solution)/shard_map/kti,io->kto/dot_general | solution.py:133
  92.5 4.8 %all-to-all-start.2 = ((bf16[4,136,144]{2,1,0:T(8,128)(2,1)}), bf16[4,136,144]{2,1,0:T(8,128)(2,1)S(1)}, u32[]{:S(2)}, u32[]{:S(2)}) async-start(bf16[4,136,144]{2,1,0:T(8,128)(2,1)} %convolution_convert_fusion), calls=%async_computation.2 | async-start | bytes 557056 | tf_op jit(solution)/shard_map/all_to_all | solution.py:136
  97.3 3.9 %fusion.5 = bf16[4,136,1024]{2,1,0:T(8,128)(2,1)} fusion(bf16[4,136,1024]{2,1,0:T(8,128)(2,1)S(1)} %all-to-all-done, bf16[1024,1168]{1,0:T(8,128)(2,1)} %all-gather.2.cloned.1.call-done), kind=kOutput, calls=%fused_computation.6 | convolution fusion | flops 1141407744 | bytes 4325376 | tf_op jit(solution)/shard_map/kti,io->kto/dot_general | solution.py:137
  102.0 7.1 %all-to-all-start.1 = ((bf16[4,136,1024]{2,1,0:T(8,128)(2,1)}), bf16[4,136,1024]{2,1,0:T(8,128)(2,1)S(1)}, u32[]{:S(2)}, u32[]{:S(2)}) async-start(bf16[4,136,1024]{2,1,0:T(8,128)(2,1)} %fusion.5), calls=%async_computation.1 | async-start | bytes 2228224 | tf_op jit(solution)/shard_map/all_to_all | solution.py:140
  109.2 1.9 %collective-permute-start.1 = (bf16[128,128]{1,0:T(8,128)(2,1)S(1)}, bf16[128,128]{1,0:T(8,128)(2,1)S(1)}, u32[]{:S(2)}, u32[]{:S(2)}) collective-permute-start(bf16[128,128]{1,0:T(8,128)(2,1)S(1)} %multiply_convert_fusion.6), channel_id=1, source_target_pairs={{4,0},{0,1},{5,2},{1,3},{6,4},{2,5},{7,6},{3,7},{12,8},{8,9},{13,1... | collective-permute-start | bytes 98312 | tf_op jit(solution)/shard_map/ppermute | solution.py:169
  111.1 3.8 %collective-permute-start.2 = (bf16[128,128]{1,0:T(8,128)(2,1)S(1)}, bf16[128,128]{1,0:T(8,128)(2,1)S(1)}, u32[]{:S(2)}, u32[]{:S(2)}) collective-permute-start(bf16[128,128]{1,0:T(8,128)(2,1)S(1)} %multiply_convert_fusion.6), channel_id=1, source_target_pairs={{0,0},{4,1},{1,2},{5,3},{2,4},{6,5},{3,6},{7,7},{8,8},{12,9},{9,10... | collective-permute-start | bytes 98312 | tf_op jit(solution)/shard_map/ppermute | solution.py:168
  115.6 1.7 all-to-all-done.1
  119.1 3.4 %all-to-all-start.3 = ((bf16[4,264,128]{2,1,0:T(8,128)(2,1)}), bf16[4,264,128]{2,1,0:T(8,128)(2,1)S(1)}, u32[]{:S(2)}, u32[]{:S(2)}) async-start(bf16[4,264,128]{2,1,0:T(8,128)(2,1)} %pad_maximum_fusion.1), calls=%async_computation.3 | async-start | bytes 540672 | tf_op jit(solution)/shard_map/all_to_all | solution.py:41
  122.8 8.6 %all-to-all-done.3 = bf16[4,264,128]{2,1,0:T(8,128)(2,1)S(1)} async-done(((bf16[4,264,128]{2,1,0:T(8,128)(2,1)}), bf16[4,264,128]{2,1,0:T(8,128)(2,1)S(1)}, u32[]{:S(2)}, u32[]{:S(2)}) %all-to-all-start.3) | async-done | bytes 270368 | tf_op jit(solution)/shard_map/all_to_all | solution.py:41
  132.1 1.2 convolution_bitcast_fusion.1
  133.9 22.0 %all_gather.8 = bf16[4,264,128]{2,1,0:T(8,128)(2,1)S(1)} all-gather(bf16[1,264,128]{2,1,0:T(8,128)(2,1)S(1)} %copy.142), channel_id=1, replica_groups=mesh['dp'=4,'ch'=4,'cl'=4,'mp'=8] {'ch'}, dimensions={0}, use_global_device_ids=true | all-gather | bytes 337920 | tf_op jit(solution)/shard_map/all_gather | solution.py:56
  158.4 3.5 %all-to-all-start.4 = ((bf16[4,256,128]{2,1,0:T(8,128)(2,1)}), bf16[4,256,128]{2,1,0:T(8,128)(2,1)S(1)}, u32[]{:S(2)}, u32[]{:S(2)}) async-start(bf16[4,256,128]{2,1,0:T(8,128)(2,1)} %copy.143), calls=%async_computation.4 | async-start | bytes 524288 | tf_op jit(solution)/shard_map/all_to_all | solution.py:66
  163.7 5.0 %all-to-all-done.4 = bf16[4,256,128]{2,1,0:T(8,128)(2,1)S(1)} async-done(((bf16[4,256,128]{2,1,0:T(8,128)(2,1)}), bf16[4,256,128]{2,1,0:T(8,128)(2,1)S(1)}, u32[]{:S(2)}, u32[]{:S(2)}) %all-to-all-start.4) | async-done | bytes 262176 | tf_op jit(solution)/shard_map/all_to_all | solution.py:66
  (91 shorter events, 12.9 us)
Async XLA Ops:
  7.2 83.1 %all-gather.2.cloned.1.call-start = ((), (), s32[]{:S(2)}) async-start(), calls=%async_computation.5 | async-start | bytes 2785280 | tf_op jit(solution)/shard_map/all_gather | solution.py:123
  62.1 4.3 %collective-permute-start = (bf16[8,4096]{1,0:T(8,128)(2,1)S(1)}, bf16[8,4096]{1,0:T(8,128)(2,1)S(1)}, u32[]{:S(2)}, u32[]{:S(2)}) collective-permute-start(bf16[8,4096]{1,0:T(8,128)(2,1)S(1)} %slice.197), channel_id=1, source_target_pairs={{0,8},{8,16},{16,24},{24,32},{32,40},{40,48},{48,56},{56,64},{64,7... | collective-permute-start | bytes 196616 | tf_op jit(solution)/shard_map/ppermute | solution.py:16
  66.5 6.9 %copy-start.5 = (f32[16]{0:T(128)S(1)}, f32[16]{0:T(128)}, u32[]{:S(2)}) copy-start(f32[16]{0:T(128)} %param.19) | copy-start | bytes 196
  66.5 6.9 %copy-start.3 = (f32[5,128]{1,0:T(8,128)S(1)}, f32[5,128]{1,0:T(8,128)}, u32[]{:S(2)}) copy-start(f32[5,128]{1,0:T(8,128)} %param.17) | copy-start | bytes 7684
  66.5 6.9 %copy-start = (f32[5,1024]{1,0:T(8,128)S(1)}, f32[5,1024]{1,0:T(8,128)}, u32[]{:S(2)}) copy-start(f32[5,1024]{1,0:T(8,128)} %param.16) | copy-start | bytes 61444
  67.6 14.1 %all-to-all-start = ((bf16[4,136,1024]{2,1,0:T(8,128)(2,1)}), bf16[4,136,1024]{2,1,0:T(8,128)(2,1)S(1)}, u32[]{:S(2)}, u32[]{:S(2)}) async-start(bf16[4,136,1024]{2,1,0:T(8,128)(2,1)} %bitcast.108), calls=%async_computation | async-start | bytes 2228224 | tf_op jit(solution)/shard_map/all_to_all | solution.py:130
  92.5 9.5 %all-to-all-start.2 = ((bf16[4,136,144]{2,1,0:T(8,128)(2,1)}), bf16[4,136,144]{2,1,0:T(8,128)(2,1)S(1)}, u32[]{:S(2)}, u32[]{:S(2)}) async-start(bf16[4,136,144]{2,1,0:T(8,128)(2,1)} %convolution_convert_fusion), calls=%async_computation.2 | async-start | bytes 557056 | tf_op jit(solution)/shard_map/all_to_all | solution.py:136
  101.2 13.8 %copy-start.2 = (f32[16]{0:T(128)S(1)}, f32[16]{0:T(128)}, u32[]{:S(2)}) copy-start(f32[16]{0:T(128)} %param.18) | copy-start | bytes 196
  102.0 15.3 %all-to-all-start.1 = ((bf16[4,136,1024]{2,1,0:T(8,128)(2,1)}), bf16[4,136,1024]{2,1,0:T(8,128)(2,1)S(1)}, u32[]{:S(2)}, u32[]{:S(2)}) async-start(bf16[4,136,1024]{2,1,0:T(8,128)(2,1)} %fusion.5), calls=%async_computation.1 | async-start | bytes 2228224 | tf_op jit(solution)/shard_map/all_to_all | solution.py:140
  109.2 9.0 %collective-permute-start.1 = (bf16[128,128]{1,0:T(8,128)(2,1)S(1)}, bf16[128,128]{1,0:T(8,128)(2,1)S(1)}, u32[]{:S(2)}, u32[]{:S(2)}) collective-permute-start(bf16[128,128]{1,0:T(8,128)(2,1)S(1)} %multiply_convert_fusion.6), channel_id=1, source_target_pairs={{4,0},{0,1},{5,2},{1,3},{6,4},{2,5},{7,6},{3,7},{12,8},{8,9},{13,1... | collective-permute-start | bytes 98312 | tf_op jit(solution)/shard_map/ppermute | solution.py:169
  111.1 7.1 %collective-permute-start.2 = (bf16[128,128]{1,0:T(8,128)(2,1)S(1)}, bf16[128,128]{1,0:T(8,128)(2,1)S(1)}, u32[]{:S(2)}, u32[]{:S(2)}) collective-permute-start(bf16[128,128]{1,0:T(8,128)(2,1)S(1)} %multiply_convert_fusion.6), channel_id=1, source_target_pairs={{0,0},{4,1},{1,2},{5,3},{2,4},{6,5},{3,6},{7,7},{8,8},{12,9},{9,10... | collective-permute-start | bytes 98312 | tf_op jit(solution)/shard_map/ppermute | solution.py:168
  119.1 12.4 %all-to-all-start.3 = ((bf16[4,264,128]{2,1,0:T(8,128)(2,1)}), bf16[4,264,128]{2,1,0:T(8,128)(2,1)S(1)}, u32[]{:S(2)}, u32[]{:S(2)}) async-start(bf16[4,264,128]{2,1,0:T(8,128)(2,1)} %pad_maximum_fusion.1), calls=%async_computation.3 | async-start | bytes 540672 | tf_op jit(solution)/shard_map/all_to_all | solution.py:41
  133.9 28.7 %copy-start.1 = (f32[1024]{0:T(1024)S(1)}, f32[1024]{0:T(1024)}, u32[]{:S(2)}) copy-start(f32[1024]{0:T(1024)} %param.21) | copy-start | bytes 12292
  158.4 10.3 %copy-start.4 = (f32[16]{0:T(128)S(1)}, f32[16]{0:T(128)}, u32[]{:S(2)}) copy-start(f32[16]{0:T(128)} %param.20) | copy-start | bytes 196
  158.4 10.3 %all-to-all-start.4 = ((bf16[4,256,128]{2,1,0:T(8,128)(2,1)}), bf16[4,256,128]{2,1,0:T(8,128)(2,1)S(1)}, u32[]{:S(2)}, u32[]{:S(2)}) async-start(bf16[4,256,128]{2,1,0:T(8,128)(2,1)} %copy.143), calls=%async_computation.4 | async-start | bytes 524288 | tf_op jit(solution)/shard_map/all_to_all | solution.py:66
Sparse Core Ops, SparseCore 0:
  10.7 79.5 all-gather.1
where the time goes:
time: 178 us; the launch traced here: 177 us
  blocking collectives  67.7 us (38%)
  waiting for transfers between devices  35.6 us (20%)
  starting transfers between devices  32.1 us (18%)
  between operations  14.5 us (8%)
  matrix products  13.8 us (8%)
  local copies, waits for them, and re-layouts  7.35 us (4%)
  other arithmetic  5.94 us (3%)
    psum x2, blocking collectives, shards(): totals = lax.psum(lax.psum(powers, CTX), 'dp')  45.7 us
    all_gather x1, blocking collectives, entering(): lax.all_gather(summary.astype(jnp.bfloat16), 'ch').astype(jnp.float32)  22 us
    all_to_all x1, waiting for transfers between devices, entering(): incoming = lax.all_to_all(outgoing, 'cl', 0, 0).astype(jnp.float32)  8.64 us
    all_gather x1, waiting for transfers between devices, shards(): panel = lax.all_gather(local_panel, CTX, axis=0, tiled=True)  8.63 us
    all_to_all x1, waiting for transfers between devices, shards(): incoming = lax.all_to_all(outgoing, 'dp', 0, 0)  8.2 us
    all_to_all x1, starting transfers between devices, shards(): x_back = lax.all_to_all(x_partials.astype(jnp.bfloat16), 'dp', 0, 0)  7.06 us
    all_to_all x1, starting transfers between devices, shards(): incoming = lax.all_to_all(outgoing, 'dp', 0, 0)  5.79 us
    all_to_all x1, waiting for transfers between devices, entering(): returned = lax.all_to_all(carried.astype(jnp.bfloat16), 'cl', 0, 0)  5.05 us
  transfers between devices with their start and end apart: 9, of which 7 were waited for; matrix products, arithmetic and copies ran while one was open for 9% of the time, Pallas kernels for 0%

commit v1 on v0

--- a/solution.py
+++ b/solution.py
@@ -120,7 +120,9 @@
     totals, rotated = lax.optimization_barrier((totals, rotated))
     kurtosis = kurtosis_from(totals, row_count)
     local_panel = jnp.concatenate([x_weight, bc_weight, dt_weight], 1)
-    panel = lax.all_gather(local_panel, CTX, axis=0, tiled=True)
+    panel = jnp.concatenate(
+        lax.all_to_all(jnp.stack([local_panel] * lax.axis_size(CTX)), CTX, 0, 0), axis=0
+    )
     seqs = lax.axis_size("dp")
     share = model_width // seqs
     rim = 8

time: 178 us -> 273 us (1.53)
  the two profiles are of different devices: /device:TPU:12 before, /device:TPU:16 now
where the time goes in v1:
time: 273 us; the launch traced here: 272 us
  waiting for transfers between devices  138 us (51%)
  blocking collectives  71.1 us (26%)
  starting transfers between devices  35.6 us (13%)
  matrix products  13.6 us (5%)
  local copies, waits for them, and re-layouts  8.5 us (3%)
  other arithmetic  4.33 us (2%)
    all_to_all x1, waiting for transfers between devices, shards(): lax.all_to_all(jnp.stack([local_panel] * lax.axis_size(CTX)), CTX, 0, 0)  103 us
    psum x2, blocking collectives, shards(): totals = lax.psum(lax.psum(powers, CTX), 'dp')  47.6 us
    all_gather x1, blocking collectives, entering(): lax.all_gather(summary.astype(jnp.bfloat16), 'ch').astype(jnp.float32)  23.4 us
    all_to_all x1, waiting for transfers between devices, shards(): incoming = lax.all_to_all(outgoing, 'dp', 0, 0)  11.1 us
    all_to_all x1, starting transfers between devices, shards(): lax.all_to_all(jnp.stack([local_panel] * lax.axis_size(CTX)), CTX, 0, 0)  10.6 us
    all_to_all x1, waiting for transfers between devices, shards(): x_back = lax.all_to_all(x_partials.astype(jnp.bfloat16), 'dp', 0, 0)  6.94 us
    all_to_all x1, waiting for transfers between devices, entering(): incoming = lax.all_to_all(outgoing, 'cl', 0, 0).astype(jnp.float32)  6.57 us
  transfers between devices with their start and end apart: 9, of which 7 were waited for; matrix products, arithmetic and copies ran while one was open for 3% of the time, Pallas kernels for 0%

profile of v1, /device:TPU:16, one launch (start us, length us, event | category | flops | bytes accessed | tf_op | source)
XLA Modules:
  0.0 272.3 jit_solution(4776929350491539314)
XLA Ops:
  0.6 1.6 copy.123
  3.2 3.3 %multiply_convert_fusion = bf16[128,64,64]{0,2,1:T(8,128)(2,1)S(1)} fusion(f32[128,64,64]{0,1,2:T(8,128)S(1)} %convolution_bitcast_fusion), kind=kOutput, calls=%fused_computation.4 | convolution fusion | flops 403791872 | bytes 3145728 | tf_op jit(solution)/shard_map/tcb,bd->tcd/dot_general | solution.py:102
  6.8 37.0 %psum.14 = f32[4,512]{1,0:T(4,128)S(1)} all-reduce(f32[4,512]{1,0:T(4,128)S(1)} %pad_maximum_fusion.3), channel_id=1, replica_groups=mesh['dp'=4,'ch'=4,'cl'=4,'mp'=8] {'ch','cl'}, use_global_device_ids=true, to_apply=%region_4.0 | all-reduce | flops 2048 | bytes 16384 | tf_op jit(solution)/shard_map/psum | solution.py:119
  43.9 10.6 %psum.15 = f32[4,512]{1,0:T(4,128)S(1)} all-reduce(f32[4,512]{1,0:T(4,128)S(1)} %psum.14), channel_id=1, replica_groups=mesh['dp'=4,'ch'=4,'cl'=4,'mp'=8] {'dp'}, use_global_device_ids=true, to_apply=%region_5.0 | all-reduce | flops 2048 | bytes 16384 | tf_op jit(solution)/shard_map/psum | solution.py:119
  55.0 1.7 collective-permute-start
  56.7 1.9 collective-permute-done
  59.8 3.5 %all-to-all-start = ((bf16[4,136,1024]{2,1,0:T(8,128)(2,1)}), bf16[4,136,1024]{2,1,0:T(8,128)(2,1)S(1)}, u32[]{:S(2)}, u32[]{:S(2)}) async-start(bf16[4,136,1024]{2,1,0:T(8,128)(2,1)} %bitcast.109), calls=%async_computation | async-start | bytes 2228224 | tf_op jit(solution)/shard_map/all_to_all | solution.py:132
  63.5 11.1 %all-to-all-done = bf16[4,136,1024]{2,1,0:T(8,128)(2,1)S(1)} async-done(((bf16[4,136,1024]{2,1,0:T(8,128)(2,1)}), bf16[4,136,1024]{2,1,0:T(8,128)(2,1)S(1)}, u32[]{:S(2)}, u32[]{:S(2)}) %all-to-all-start) | async-done | bytes 1114144 | tf_op jit(solution)/shard_map/all_to_all | solution.py:132
  74.5 1.8 stack.17
  76.4 10.6 %all-to-all-start.1 = ((bf16[16,64,1168]{2,1,0:T(8,128)(2,1)}), bf16[16,64,1168]{2,1,0:T(8,128)(2,1)S(1)}, u32[]{:S(2)}, u32[]{:S(2)}) async-start(bf16[16,64,1168]{2,1,0:T(8,128)(2,1)} %stack.17), calls=%async_computation.1 | async-start | bytes 5242880 | tf_op jit(solution)/shard_map/all_to_all | solution.py:124
  87.2 103.3 %all-to-all-done.1 = bf16[16,64,1168]{2,1,0:T(8,128)(2,1)S(1)} async-done(((bf16[16,64,1168]{2,1,0:T(8,128)(2,1)}), bf16[16,64,1168]{2,1,0:T(8,128)(2,1)S(1)}, u32[]{:S(2)}, u32[]{:S(2)}) %all-to-all-start.1) | async-done | bytes 2392096 | tf_op jit(solution)/shard_map/all_to_all | solution.py:124
  190.5 2.4 convolution_convert_fusion
  192.9 3.4 %all-to-all-start.3 = ((bf16[4,136,144]{2,1,0:T(8,128)(2,1)}), bf16[4,136,144]{2,1,0:T(8,128)(2,1)S(1)}, u32[]{:S(2)}, u32[]{:S(2)}) async-start(bf16[4,136,144]{2,1,0:T(8,128)(2,1)} %convolution_convert_fusion), calls=%async_computation.3 | async-start | bytes 557056 | tf_op jit(solution)/shard_map/all_to_all | solution.py:138
  196.3 3.6 %fusion.5 = bf16[4,136,1024]{2,1,0:T(8,128)(2,1)} fusion(bf16[4,136,1024]{2,1,0:T(8,128)(2,1)} %copy-done, bf16[1024,1168]{1,0:T(8,128)(2,1)S(1)} %bitcast.116), kind=kOutput, calls=%fused_computation.6 | convolution fusion | flops 1141407744 | bytes 4325376 | tf_op jit(solution)/shard_map/kti,io->kto/dot_general | solution.py:139
  199.9 3.2 %all-to-all-done.3 = bf16[4,136,144]{2,1,0:T(8,128)(2,1)S(1)} async-done(((bf16[4,136,144]{2,1,0:T(8,128)(2,1)}), bf16[4,136,144]{2,1,0:T(8,128)(2,1)S(1)}, u32[]{:S(2)}, u32[]{:S(2)}) %all-to-all-start.3) | async-done | bytes 156704 | tf_op jit(solution)/shard_map/all_to_all | solution.py:138
  203.1 3.5 %all-to-all-start.2 = ((bf16[4,136,1024]{2,1,0:T(8,128)(2,1)}), bf16[4,136,1024]{2,1,0:T(8,128)(2,1)S(1)}, u32[]{:S(2)}, u32[]{:S(2)}) async-start(bf16[4,136,1024]{2,1,0:T(8,128)(2,1)} %fusion.5), calls=%async_computation.2 | async-start | bytes 2228224 | tf_op jit(solution)/shard_map/all_to_all | solution.py:142
  206.7 2.2 collective-permute-start.1
  209.0 1.9 collective-permute-start.2
  211.6 6.9 %all-to-all-done.2 = bf16[4,136,1024]{2,1,0:T(8,128)(2,1)S(1)} async-done(((bf16[4,136,1024]{2,1,0:T(8,128)(2,1)}), bf16[4,136,1024]{2,1,0:T(8,128)(2,1)S(1)}, u32[]{:S(2)}, u32[]{:S(2)}) %all-to-all-start.2) | async-done | bytes 1114144 | tf_op jit(solution)/shard_map/all_to_all | solution.py:142
  220.3 5.1 %all-to-all-start.4 = ((bf16[4,264,128]{2,1,0:T(8,128)(2,1)}), bf16[4,264,128]{2,1,0:T(8,128)(2,1)S(1)}, u32[]{:S(2)}, u32[]{:S(2)}) async-start(bf16[4,264,128]{2,1,0:T(8,128)(2,1)} %pad_maximum_fusion.1), calls=%async_computation.4 | async-start | bytes 540672 | tf_op jit(solution)/shard_map/all_to_all | solution.py:41
  225.7 6.6 %all-to-all-done.4 = bf16[4,264,128]{2,1,0:T(8,128)(2,1)S(1)} async-done(((bf16[4,264,128]{2,1,0:T(8,128)(2,1)}), bf16[4,264,128]{2,1,0:T(8,128)(2,1)S(1)}, u32[]{:S(2)}, u32[]{:S(2)}) %all-to-all-start.4) | async-done | bytes 270368 | tf_op jit(solution)/shard_map/all_to_all | solution.py:41
  234.6 23.4 %all_gather.4 = bf16[4,264,128]{2,1,0:T(8,128)(2,1)S(1)} all-gather(bf16[1,264,128]{2,1,0:T(8,128)(2,1)S(1)} %copy.142), channel_id=1, replica_groups=mesh['dp'=4,'ch'=4,'cl'=4,'mp'=8] {'ch'}, dimensions={0}, use_global_device_ids=true | all-gather | bytes 337920 | tf_op jit(solution)/shard_map/all_gather | solution.py:56
  260.7 3.5 %all-to-all-start.5 = ((bf16[4,256,128]{2,1,0:T(8,128)(2,1)}), bf16[4,256,128]{2,1,0:T(8,128)(2,1)S(1)}, u32[]{:S(2)}, u32[]{:S(2)}) async-start(bf16[4,256,128]{2,1,0:T(8,128)(2,1)} %copy.143), calls=%async_computation.5 | async-start | bytes 524288 | tf_op jit(solution)/shard_map/all_to_all | solution.py:66
  265.9 5.0 %all-to-all-done.5 = bf16[4,256,128]{2,1,0:T(8,128)(2,1)S(1)} async-done(((bf16[4,256,128]{2,1,0:T(8,128)(2,1)}), bf16[4,256,128]{2,1,0:T(8,128)(2,1)S(1)}, u32[]{:S(2)}, u32[]{:S(2)}) %all-to-all-start.5) | async-done | bytes 262176 | tf_op jit(solution)/shard_map/all_to_all | solution.py:66
  (99 shorter events, 13.7 us)
Async XLA Ops:
  55.0 3.6 %collective-permute-start = (bf16[8,4096]{1,0:T(8,128)(2,1)S(1)}, bf16[8,4096]{1,0:T(8,128)(2,1)S(1)}, u32[]{:S(2)}, u32[]{:S(2)}) collective-permute-start(bf16[8,4096]{1,0:T(8,128)(2,1)S(1)} %slice.197), channel_id=1, source_target_pairs={{0,8},{8,16},{16,24},{24,32},{32,40},{40,48},{48,56},{56,64},{64,7... | collective-permute-start | bytes 196616 | tf_op jit(solution)/shard_map/ppermute | solution.py:16
  58.7 4.6 %copy-start.4 = (bf16[64,16]{0,1:T(8,128)(2,1)S(1)}, bf16[64,16]{0,1:T(8,128)(2,1)}, u32[]{:S(2)}) copy-start(bf16[64,16]{0,1:T(8,128)(2,1)} %param.15) | copy-start | bytes 6148
  58.7 4.7 %copy-start.1 = (bf16[64,1024]{1,0:T(8,128)(2,1)S(1)}, bf16[64,1024]{1,0:T(8,128)(2,1)}, u32[]{:S(2)}) copy-start(bf16[64,1024]{1,0:T(8,128)(2,1)} %param.13) | copy-start | bytes 393220
  58.7 4.7 %copy-start.2 = (bf16[64,128]{1,0:T(8,128)(2,1)S(1)}, bf16[64,128]{1,0:T(8,128)(2,1)}, u32[]{:S(2)}) copy-start(bf16[64,128]{1,0:T(8,128)(2,1)} %param.14) | copy-start | bytes 49156
  59.8 14.7 %all-to-all-start = ((bf16[4,136,1024]{2,1,0:T(8,128)(2,1)}), bf16[4,136,1024]{2,1,0:T(8,128)(2,1)S(1)}, u32[]{:S(2)}, u32[]{:S(2)}) async-start(bf16[4,136,1024]{2,1,0:T(8,128)(2,1)} %bitcast.109), calls=%async_computation | async-start | bytes 2228224 | tf_op jit(solution)/shard_map/all_to_all | solution.py:132
  74.5 1.8 copy-start
  76.4 10.7 %copy-start.9 = (f32[16]{0:T(128)S(1)}, f32[16]{0:T(128)}, u32[]{:S(2)}) copy-start(f32[16]{0:T(128)} %param.19) | copy-start | bytes 196
  76.4 10.7 %copy-start.7 = (f32[5,128]{1,0:T(8,128)S(1)}, f32[5,128]{1,0:T(8,128)}, u32[]{:S(2)}) copy-start(f32[5,128]{1,0:T(8,128)} %param.17) | copy-start | bytes 7684
  76.4 10.7 %copy-start.3 = (f32[5,1024]{1,0:T(8,128)S(1)}, f32[5,1024]{1,0:T(8,128)}, u32[]{:S(2)}) copy-start(f32[5,1024]{1,0:T(8,128)} %param.16) | copy-start | bytes 61444
  76.4 114.1 %all-to-all-start.1 = ((bf16[16,64,1168]{2,1,0:T(8,128)(2,1)}), bf16[16,64,1168]{2,1,0:T(8,128)(2,1)S(1)}, u32[]{:S(2)}, u32[]{:S(2)}) async-start(bf16[16,64,1168]{2,1,0:T(8,128)(2,1)} %stack.17), calls=%async_computation.1 | async-start | bytes 5242880 | tf_op jit(solution)/shard_map/all_to_all | solution.py:124
  192.9 10.2 %all-to-all-start.3 = ((bf16[4,136,144]{2,1,0:T(8,128)(2,1)}), bf16[4,136,144]{2,1,0:T(8,128)(2,1)S(1)}, u32[]{:S(2)}, u32[]{:S(2)}) async-start(bf16[4,136,144]{2,1,0:T(8,128)(2,1)} %convolution_convert_fusion), calls=%async_computation.3 | async-start | bytes 557056 | tf_op jit(solution)/shard_map/all_to_all | solution.py:138
  199.9 11.1 %copy-start.6 = (f32[16]{0:T(128)S(1)}, f32[16]{0:T(128)}, u32[]{:S(2)}) copy-start(f32[16]{0:T(128)} %param.18) | copy-start | bytes 196
  203.1 15.4 %all-to-all-start.2 = ((bf16[4,136,1024]{2,1,0:T(8,128)(2,1)}), bf16[4,136,1024]{2,1,0:T(8,128)(2,1)S(1)}, u32[]{:S(2)}, u32[]{:S(2)}) async-start(bf16[4,136,1024]{2,1,0:T(8,128)(2,1)} %fusion.5), calls=%async_computation.2 | async-start | bytes 2228224 | tf_op jit(solution)/shard_map/all_to_all | solution.py:142
  206.7 12.6 %collective-permute-start.1 = (bf16[128,128]{1,0:T(8,128)(2,1)S(1)}, bf16[128,128]{1,0:T(8,128)(2,1)S(1)}, u32[]{:S(2)}, u32[]{:S(2)}) collective-permute-start(bf16[128,128]{1,0:T(8,128)(2,1)S(1)} %multiply_convert_fusion.6), channel_id=1, source_target_pairs={{4,0},{0,1},{5,2},{1,3},{6,4},{2,5},{7,6},{3,7},{12,8},{8,9},{13,1... | collective-permute-start | bytes 98312 | tf_op jit(solution)/shard_map/ppermute | solution.py:171
  209.0 10.4 %collective-permute-start.2 = (bf16[128,128]{1,0:T(8,128)(2,1)S(1)}, bf16[128,128]{1,0:T(8,128)(2,1)S(1)}, u32[]{:S(2)}, u32[]{:S(2)}) collective-permute-start(bf16[128,128]{1,0:T(8,128)(2,1)S(1)} %multiply_convert_fusion.6), channel_id=1, source_target_pairs={{0,0},{4,1},{1,2},{5,3},{2,4},{6,5},{3,6},{7,7},{8,8},{12,9},{9,10... | collective-permute-start | bytes 98312 | tf_op jit(solution)/shard_map/ppermute | solution.py:170
  220.3 11.9 %all-to-all-start.4 = ((bf16[4,264,128]{2,1,0:T(8,128)(2,1)}), bf16[4,264,128]{2,1,0:T(8,128)(2,1)S(1)}, u32[]{:S(2)}, u32[]{:S(2)}) async-start(bf16[4,264,128]{2,1,0:T(8,128)(2,1)} %pad_maximum_fusion.1), calls=%async_computation.4 | async-start | bytes 540672 | tf_op jit(solution)/shard_map/all_to_all | solution.py:41
  234.6 30.2 %copy-start.5 = (f32[1024]{0:T(1024)S(1)}, f32[1024]{0:T(1024)}, u32[]{:S(2)}) copy-start(f32[1024]{0:T(1024)} %param.21) | copy-start | bytes 12292
  260.7 10.3 %copy-start.8 = (f32[16]{0:T(128)S(1)}, f32[16]{0:T(128)}, u32[]{:S(2)}) copy-start(f32[16]{0:T(128)} %param.20) | copy-start | bytes 196
  260.7 10.3 %all-to-all-start.5 = ((bf16[4,256,128]{2,1,0:T(8,128)(2,1)}), bf16[4,256,128]{2,1,0:T(8,128)(2,1)S(1)}, u32[]{:S(2)}, u32[]{:S(2)}) async-start(bf16[4,256,128]{2,1,0:T(8,128)(2,1)} %copy.143), calls=%async_computation.5 | async-start | bytes 524288 | tf_op jit(solution)/shard_map/all_to_all | solution.py:66
